TPU v7x, 32 devices: a whole 2x2x4 slice. The times are simulated.
32 devices in a mesh: tile: 8 (over y, x, core), mem: 4 (over z).
Axes of the slice: x: 2, y: 2, z: 4, core: 2. Of those that a mesh axis runs over, the one named last changes fastest.
Arguments:
- control: bfloat16 [80, 1, 360, 720], P('mem', None, 'tile'), may hold values from -6 to 6
- perturb: bfloat16 [80, 1, 360, 720], P('mem', None, 'tile'), may hold values from -6 to 6
- lon_taps: bfloat16 [17], replicated, may hold values from 0.026367188 to 0.07910156
- lat_taps: bfloat16 [17], replicated, may hold values from 0.026367188 to 0.07910156
- innov: float32 [8, 8, 256], P('tile'), may hold values from -6 to 6
- inv_var: float32 [8, 8, 256], P('tile'), may hold values from 1 to 8
- cell_index: int32 [8, 8, 256], P('tile'), may hold values from 0 to 32399, as said below
- counts: int32 [8, 8], P('tile'), may hold values from 0 to 256, as said below
Outputs:
- gradient: float32 [80, 1, 360, 720], P('mem', None, 'tile')
Inputs may be any that keep to these rules, and one draw needn't show every extreme that they name: `cell_index`: an observation's cell within its owning tile, level * 45 * 720 + longitude within the tile * 720 + latitude; both ends are taken. `counts`: live slots per pair of tiles; some pair fills all 256 slots in every draw, and some owning tiles receive far more than others.
All inputs are finite; a program needn't handle non-finite values.
Results may differ from a plain program's by a relative error of at most 0.00066.
Values may be sent and summed in bfloat16 or wider, within the bound.
No kernel may reach another device: no remote copies, remote signals or barrier semaphores. Data moves between devices by JAX's collectives and lax.ppermute only.
A program may use at most 64 MiB of HBM per device.

v0:
```python
import math
import jax
import jax.numpy as jnp
from jax import lax
from jax.sharding import PartitionSpec as P


def extended_2(block, sides, width):
    for axis, dim in sides:
        count = lax.axis_size(axis)
        forward = [(i, i + 1) for i in range(count - 1)]
        forward.append((count - 1, 0))
        backward = [(target, source) for source, target in forward]
        low = lax.ppermute(
            lax.slice_in_dim(block, block.shape[dim] - width, None, axis=dim), axis, forward
        )
        high = lax.ppermute(lax.slice_in_dim(block, 0, width, axis=dim), axis, backward)
        block = jnp.concatenate([low, block, high], axis=dim)
    return block


def band_from(offsets, tap_weights):
    radius = tap_weights.shape[0] - 1
    taps = tap_weights.astype(jnp.float32)
    band = jnp.zeros(offsets.shape, jnp.float32)
    for offset in range(radius + 1):
        band = band + jnp.where(offsets == offset, taps[offset], 0.0)
    return band.astype(jnp.bfloat16)


def lon_band(tap_weights, lon_cells):
    radius = tap_weights.shape[0] - 1
    row_ids = lax.broadcasted_iota(jnp.int32, (lon_cells, lon_cells + 2 * radius), 0)
    col_ids = lax.broadcasted_iota(jnp.int32, (lon_cells, lon_cells + 2 * radius), 1)
    return band_from(jnp.abs(col_ids - row_ids - radius), tap_weights)


def lat_block_band(tap_weights, block_cells):
    radius = tap_weights.shape[0] - 1
    row_ids = lax.broadcasted_iota(jnp.int32, (block_cells + 2 * radius, block_cells), 0)
    col_ids = lax.broadcasted_iota(jnp.int32, (block_cells + 2 * radius, block_cells), 1)
    return band_from(jnp.abs(row_ids - radius - col_ids), tap_weights)


def localize(extended, band_lon, band_blocks, radius, block_cells):
    along = jnp.einsum(
        "ij,mljk->mlik", band_lon, extended, preferred_element_type=jnp.float32
    ).astype(jnp.bfloat16)
    members_here, levels, lon_cells, lat_cells = along.shape
    padded = jnp.pad(along, ((0, 0), (0, 0), (0, 0), (radius, radius)))
    block_count = lat_cells // block_cells
    windows = jnp.stack(
        [
            padded[:, :, :, block * block_cells : block * block_cells + block_cells + 2 * radius]
            for block in range(block_count)
        ],
        axis=3,
    )
    result = jnp.einsum("mlibk,kq->mlibq", windows, band_blocks, preferred_element_type=jnp.float32)
    return result.reshape(members_here, levels, lon_cells, lat_cells)


def pick_cells(field_rows, row_index, col_index, block_rows):
    row_count, col_count = field_rows.shape
    field_cols = field_rows.T

    def pick_one_block(indices):
        rows_here, cols_here = indices
        onehot_rows = (
            rows_here[:, None] == jnp.arange(row_count, dtype=jnp.int32)[None, :]
        ).astype(jnp.float32)
        onehot_cols = (
            cols_here[:, None] == jnp.arange(col_count, dtype=jnp.int32)[None, :]
        ).astype(jnp.float32)
        picked = jnp.dot(
            onehot_cols,
            field_cols,
            precision=lax.Precision.HIGHEST,
            preferred_element_type=jnp.float32,
        )
        return jnp.sum(picked * onehot_rows, axis=1)

    values = lax.map(
        pick_one_block, (row_index.reshape(-1, block_rows), col_index.reshape(-1, block_rows))
    )
    return values.reshape(-1)


def spread_cells(misfit, row_index, col_index, row_count, col_count, block_rows):

    def spread_one_block(total, items):
        rows_here, cols_here, values = items
        onehot_rows = (
            rows_here[:, None] == jnp.arange(row_count, dtype=jnp.int32)[None, :]
        ).astype(jnp.float32)
        onehot_cols = (
            cols_here[:, None] == jnp.arange(col_count, dtype=jnp.int32)[None, :]
        ).astype(jnp.float32)
        weighted = onehot_rows * values[:, None]
        return (
            total
            + jnp.dot(
                weighted.T,
                onehot_cols,
                precision=lax.Precision.HIGHEST,
                preferred_element_type=jnp.float32,
            ),
            None,
        )

    start = jnp.zeros((row_count, col_count), jnp.float32)
    items = (
        row_index.reshape(-1, block_rows),
        col_index.reshape(-1, block_rows),
        misfit.reshape(-1, block_rows),
    )
    total, _ = lax.scan(spread_one_block, start, items)
    return total


def local(control, perturb, lon_taps, lat_taps, innov, inv_var, cell_index, counts):
    members_here, levels, lon_cells, lat_cells = control.shape
    radius = lon_taps.shape[0] - 1
    block_cells = 144
    band_lon = lon_band(lon_taps, lon_cells)
    band_blocks = lat_block_band(lat_taps, block_cells)
    extended = extended_2(control, (("tile", 2),), radius)
    smoothed = localize(extended, band_lon, band_blocks, radius, block_cells)
    member_sum = jnp.sum(perturb.astype(jnp.float32) * smoothed, axis=0)
    slot_ids = lax.broadcasted_iota(jnp.int32, innov.shape, 2)
    is_live = slot_ids < counts[:, :, None]
    weights = jnp.where(is_live, inv_var, 0.0)
    received = (
        lax.all_to_all(innov, "tile", split_axis=1, concat_axis=0, tiled=True),
        lax.all_to_all(weights, "tile", split_axis=1, concat_axis=0, tiled=True),
        lax.all_to_all(cell_index, "tile", split_axis=1, concat_axis=0, tiled=True),
    )
    observed = received[0].reshape(-1)
    weight_recv = received[1].reshape(-1)
    cells_hit = received[2].reshape(-1)
    row_index = cells_hit // lat_cells
    col_index = cells_hit % lat_cells
    row_count = levels * lon_cells
    block_rows = math.gcd(observed.shape[0], 1024)
    increment = lax.psum(member_sum, "mem")
    at_cells = pick_cells(increment.reshape(row_count, lat_cells), row_index, col_index, block_rows)
    misfit = weight_recv * (at_cells - observed)
    spread = spread_cells(misfit, row_index, col_index, row_count, lat_cells, block_rows)
    spread = spread.reshape(levels, lon_cells, lat_cells)
    wide_pert = extended_2(perturb, (("tile", 2),), radius)
    wide_spread = extended_2(spread, (("tile", 1),), radius)
    wide_products = (wide_pert.astype(jnp.float32) * wide_spread[None]).astype(jnp.bfloat16)
    return control.astype(jnp.float32) + localize(
        wide_products, band_lon, band_blocks, radius, block_cells
    )


def solution(mesh):
    return jax.shard_map(
        local,
        mesh=mesh,
        in_specs=(
            P("mem", None, "tile", None),
            P("mem", None, "tile", None),
            P(),
            P(),
            P("tile", None, None),
            P("tile", None, None),
            P("tile", None, None),
            P("tile", None),
        ),
        out_specs=P("mem", None, "tile", None),
        check_vma=False,
    )
```

profile of v0, /device:TPU:11, one launch (start us, length us, event | category | flops | bytes accessed | tf_op | source)
XLA Modules:
  0.0 176.9 jit_solution(8008073635435257452)
XLA Ops:
  6.6 1.5 fusion.166
  8.1 1.8 %collective-permute-start.2 = (bf16[20,1,16,720]{3,2,0,1:T(8,128)(2,1)S(1)}, bf16[20,1,16,720]{3,2,0,1:T(8,128)(2,1)}, u32[]{:S(2)}, u32[]{:S(2)}) collective-permute-start(bf16[20,1,16,720]{3,2,0,1:T(8,128)(2,1)S(1)} %get-tuple-element.115), channel_id=1, source_target_pairs={{0,4},{4,8},{8,12},{12,16},{16,20},{20,24},{24,28},{28,0},{1,5},{5... | collective-permute-start | bytes 1382408 | tf_op jit(solution)/shard_map/ppermute | solution.py:14
  9.9 1.3 copy.48
  11.2 4.9 %all-to-all-start = ((s32[1,8,256]{2,0,1:T(1,128)}), s32[1,8,256]{2,0,1:T(1,128)S(1)}, u32[]{:S(2)}, u32[]{:S(2)}) async-start(s32[1,8,256]{2,0,1:T(1,128)} %copy.48), calls=%async_computation | async-start | bytes 16384 | tf_op jit(solution)/shard_map/all_to_all | solution.py:136
  16.1 2.2 %fusion.167 = (bf16[20,1,16,720]{3,2,0,1:T(8,128)(2,1)}, bf16[20,1,16,720]{3,2,0,1:T(8,128)(2,1)S(1)}) fusion(bf16[20,1,45,720]{3,2,0,1:T(8,128)(2,1)} %bitcast.147), kind=kLoop, calls=%fused_computation.200 | loop fusion | bytes 1843200 | tf_op jit(solution)/shard_map/slice | solution.py:15
  18.3 1.5 collective-permute-start
  23.2 4.4 %all-to-all-start.1 = ((f32[1,8,256]{2,0,1:T(1,128)}), f32[1,8,256]{2,0,1:T(1,128)S(1)}, u32[]{:S(2)}, u32[]{:S(2)}) async-start(f32[1,8,256]{2,0,1:T(1,128)} %compare_select_fusion), calls=%async_computation.1 | async-start | bytes 16384 | tf_op jit(solution)/shard_map/all_to_all | solution.py:135
  27.7 5.6 %all-to-all-done.1 = f32[1,8,256]{2,0,1:T(1,128)S(1)} async-done(((f32[1,8,256]{2,0,1:T(1,128)}), f32[1,8,256]{2,0,1:T(1,128)S(1)}, u32[]{:S(2)}, u32[]{:S(2)}) %all-to-all-start.1) | async-done | bytes 8224 | tf_op jit(solution)/shard_map/all_to_all | solution.py:135
  33.4 4.0 %all-to-all-start.2 = ((f32[1,8,256]{2,0,1:T(1,128)}), f32[1,8,256]{2,0,1:T(1,128)S(1)}, u32[]{:S(2)}, u32[]{:S(2)}) async-start(f32[1,8,256]{2,0,1:T(1,128)} %copy.57), calls=%async_computation.2 | async-start | bytes 16384 | tf_op jit(solution)/shard_map/all_to_all | solution.py:134
  37.5 3.1 %all-to-all-done.2 = f32[1,8,256]{2,0,1:T(1,128)S(1)} async-done(((f32[1,8,256]{2,0,1:T(1,128)}), f32[1,8,256]{2,0,1:T(1,128)S(1)}, u32[]{:S(2)}, u32[]{:S(2)}) %all-to-all-start.2) | async-done | bytes 8224 | tf_op jit(solution)/shard_map/all_to_all | solution.py:134
  40.7 12.1 %fusion.31 = bf16[20,1,45,720]{3,2,0,1:T(8,128)(2,1)S(1)} fusion(bf16[20,1,16,720]{3,2,0,1:T(8,128)(2,1)} %collective-permute-done.3, bf16[20,1,45,720]{3,2,0,1:T(8,128)(2,1)S(1)} %bitcast.146, bf16[20,1,16,720]{3,2,0,1:T(8,128)(2,1)} %collective-permute-done.2, f32[]{:T(128)} %bitcast.31, f32[]{:T(128)} %bitcast.30, f32[]{:T(128)} %bitcast.29, ...), kind=kOutput, calls=%fused_computation.44 | convolution fusion | flops 107279912 | bytes 3513668 | tf_op jit(solution)/shard_map/ij,mljk->mlik/dot_general | solution.py:46
  53.7 11.5 %fusion.25 = f32[20,45,5,144]{3,1,2,0:T(8,128)S(1)} fusion(f32[]{:T(128)} %bitcast.58, f32[]{:T(128)} %bitcast.57, f32[]{:T(128)} %bitcast.56, f32[]{:T(128)} %bitcast.55, f32[]{:T(128)} %bitcast.54, f32[]{:T(128)} %bitcast.53, f32[]{:T(128)} %bitcast.52, f32[]{:T(128)} %bitcast.51, f32[]{:T(128)} %bitcast.50, f32[]{:T(128)} %bitcast.49, f32[]{:T(128)} %bitcast.48, ...), kind=kOutput, calls=%fused_computation.38 | convolution fusion | flops 229439232 | bytes 4176772 | tf_op jit(solution)/shard_map/mlibk,kq->mlibq/dot_general | solution.py:59
  65.2 6.4 %copy.55 = f32[20,45,5,144]{3,2,1,0:T(8,128)} copy(f32[20,45,5,144]{3,1,2,0:T(8,128)S(1)} %fusion.25) | data formatting | bytes 5184000 | tf_op jit(solution)/shard_map/mlibk,kq->mlibq/dot_general | solution.py:59
  71.6 4.9 %reshape.136 = f32[20,1,45,720]{3,2,0,1:T(8,128)S(1)} reshape(f32[20,45,5,144]{3,2,1,0:T(8,128)} %copy.55) | data formatting | bytes 5184000 | tf_op jit(solution)/shard_map/reshape | solution.py:60
  76.4 2.4 %multiply_reduce_fusion = f32[45,720]{1,0:T(8,128)} fusion(f32[20,1,45,720]{3,2,0,1:T(8,128)S(1)} %reshape.136, bf16[20,1,45,720]{3,2,1,0:T(8,128)(2,1)} %param.13), kind=kLoop, calls=%fused_computation.22 | loop fusion | flops 1911600 | bytes 4017600 | tf_op jit(solution)/shard_map/reduce_sum | solution.py:129
  78.9 32.7 %all-reduce.4.cloned.1.call-done = f32[720,45]{0,1:T(8,128)} async-done(((f32[720,45]{0,1:T(8,128)}), f32[720,45]{0,1:T(8,128)}) %all-reduce.4.cloned.1.call-update) | async-done | bytes 129616 | tf_op jit(solution)/shard_map/psum | solution.py:145
  111.6 1.1 copy.56
  112.7 3.8 %while.21 = (s32[]{:T(128)}, f32[2,1024]{1,0:T(2,128)S(1)}, s32[2,1024]{1,0:T(2,128)S(1)}, s32[2,1024]{1,0:T(2,128)S(1)}, f32[720,45]{1,0:T(8,128)S(1)}, /*index=5*/s32[]{:T(128)}, s32[]{:T(128)}) while((s32[]{:T(128)}, f32[2,1024]{1,0:T(2,128)S(1)}, s32[2,1024]{1,0:T(2,128)S(1)}, s32[2,1024]{1,0:T(2,128)S(1)}, f32[720,45]{1,0:T(8,128)S(1)}, ...), condition=%wide.region_4.5_spmd, body=%wide.region_2.4_spmd.sunk | while | flops 399005696 | bytes 166549 | solution.py:83
  112.7 1.8 %fusion.179 = f32[1024]{0:T(1024)S(1)} fusion(f32[720,45]{1,0:T(8,128)S(1)} %get-tuple-element.245, s32[1024]{0:T(1024)S(1)} %bitcast.156, s32[1024]{0:T(1024)S(1)} %bitcast.157), kind=kOutput, calls=%fused_computation.4.clone.1 | convolution fusion | flops 399005696 | bytes 141888 | tf_op jit(solution)/shard_map/while/body/eval_jaxpr/dot_general | solution.py:75
  114.6 1.8 %fusion.179 = f32[1024]{0:T(1024)S(1)} fusion(f32[720,45]{1,0:T(8,128)S(1)} %get-tuple-element.245, s32[1024]{0:T(1024)S(1)} %bitcast.156, s32[1024]{0:T(1024)S(1)} %bitcast.157), kind=kOutput, calls=%fused_computation.4.clone.1 | convolution fusion | flops 399005696 | bytes 141888 | tf_op jit(solution)/shard_map/while/body/eval_jaxpr/dot_general | solution.py:75
  116.5 3.1 %while.22 = (s32[]{:T(128)}, f32[45,720]{1,0:T(8,128)S(1)}, s32[2,1024]{1,0:T(2,128)S(1)}, f32[2,1024]{1,0:T(2,128)S(1)}, s32[2,1024]{1,0:T(2,128)S(1)}, /*index=5*/s32[]{:T(128)}, s32[]{:T(128)}) while((s32[]{:T(128)}, f32[45,720]{1,0:T(8,128)S(1)}, s32[2,1024]{1,0:T(2,128)S(1)}, f32[2,1024]{1,0:T(2,128)S(1)}, ...), condition=%wide.region_6.7_spmd.clone, body=%wide.region_5.6_spmd.clone.sunk | while | flops 399025440 | bytes 296159 | solution.py:117
  116.6 1.5 fusion.181
  118.1 1.5 fusion.181
  119.7 3.9 %collective-permute-start.4 = (f32[1,16,720]{2,1,0:T(8,128)S(1)}, f32[1,16,720]{2,1,0:T(8,128)S(1)}, u32[]{:S(2)}, u32[]{:S(2)}) collective-permute-start(f32[1,16,720]{2,1,0:T(8,128)S(1)} %get-tuple-element.119), channel_id=1, source_target_pairs={{0,4},{4,8},{8,12},{12,16},{16,20},{20,24},{24,28},{28,0},{1,5},{5... | collective-permute-start | bytes 138248 | tf_op jit(solution)/shard_map/ppermute | solution.py:14
  123.6 1.2 collective-permute-done.4
  124.7 3.2 %collective-permute-done.5 = f32[1,16,720]{2,1,0:T(8,128)S(1)} collective-permute-done((f32[1,16,720]{2,1,0:T(8,128)S(1)}, f32[1,16,720]{2,1,0:T(8,128)S(1)}, u32[]{:S(2)}, u32[]{:S(2)}) %collective-permute-start.5) | collective-permute-done | bytes 46112 | tf_op jit(solution)/shard_map/ppermute | solution.py:17
  128.0 12.3 %fusion.30 = bf16[20,1,45,720]{3,2,0,1:T(8,128)(2,1)S(1)} fusion(bf16[20,16,720]{2,1,0:T(8,128)(2,1)} %bitcast.8, bf16[20,45,720]{2,1,0:T(8,128)(2,1)S(1)} %bitcast.148, bf16[20,16,720]{2,1,0:T(8,128)(2,1)} %bitcast.5, f32[77,720]{1,0:T(8,128)S(1)} %maximum_bitcast_fusion.6, f32[]{:T(128)} %bitcast.31, f32[]{:T(128)} %bitcast.30, f32[]{:T(128)} %bitcast.29, ...), kind=kOutput, calls=%fused_computation.43 | convolution fusion | flops 109497512 | bytes 3735428 | tf_op jit(solution)/shard_map/ij,mljk->mlik/dot_general | solution.py:46
  141.2 11.5 %fusion.23 = f32[20,45,5,144]{3,1,2,0:T(8,128)S(1)} fusion(f32[]{:T(128)} %bitcast.58, f32[]{:T(128)} %bitcast.57, f32[]{:T(128)} %bitcast.56, f32[]{:T(128)} %bitcast.55, f32[]{:T(128)} %bitcast.54, f32[]{:T(128)} %bitcast.53, f32[]{:T(128)} %bitcast.52, f32[]{:T(128)} %bitcast.51, f32[]{:T(128)} %bitcast.50, f32[]{:T(128)} %bitcast.49, f32[]{:T(128)} %bitcast.48, ...), kind=kOutput, calls=%fused_computation.36 | convolution fusion | flops 229439232 | bytes 4176772 | tf_op jit(solution)/shard_map/mlibk,kq->mlibq/dot_general | solution.py:59
  152.7 6.4 %copy.59 = f32[20,45,5,144]{3,2,1,0:T(8,128)} copy(f32[20,45,5,144]{3,1,2,0:T(8,128)S(1)} %fusion.23) | data formatting | bytes 5184000 | tf_op jit(solution)/shard_map/mlibk,kq->mlibq/dot_general | solution.py:59
  159.1 4.9 %reshape.141 = f32[20,1,45,720]{3,2,0,1:T(8,128)S(1)} reshape(f32[20,45,5,144]{3,2,1,0:T(8,128)} %copy.59) | data formatting | bytes 5184000 | tf_op jit(solution)/shard_map/reshape | solution.py:60
  164.0 1.7 convert_add_fusion
  165.7 4.4 %copy.60 = f32[20,1,45,720]{3,1,2,0:T(1,128)} copy(f32[20,1,45,720]{3,2,0,1:T(8,128)S(1)} %convert_add_fusion) | data formatting | bytes 5184000 | tf_op jit(solution)/shard_map/add | solution.py:153
  (64 shorter events, 5.7 us)
Async XLA Ops:
  6.5 34.1 %copy-start = (bf16[20,1,45,720]{3,2,1,0:T(8,128)(2,1)S(1)}, bf16[20,1,45,720]{3,2,1,0:T(8,128)(2,1)}, u32[]{:S(2)}) copy-start(bf16[20,1,45,720]{3,2,1,0:T(8,128)(2,1)} %param.12) | copy-start | bytes 3888004
  6.5 13.2 %copy-start.7 = (s32[1,8]{1,0:T(1,128)S(1)}, s32[1,8]{1,0:T(1,128)}, u32[]{:S(2)}) copy-start(s32[1,8]{1,0:T(1,128)} %param.19) | copy-start | bytes 100
  6.5 13.2 %copy-start.5 = (f32[1,8,256]{2,1,0:T(8,128)S(1)}, f32[1,8,256]{2,1,0:T(8,128)}, u32[]{:S(2)}) copy-start(f32[1,8,256]{2,1,0:T(8,128)} %param.17) | copy-start | bytes 24580
  6.5 13.9 %copy-start.3 = (bf16[17]{0:T(256)(128)(2,1)S(1)}, bf16[17]{0:T(256)(128)(2,1)}, u32[]{:S(2)}) copy-start(bf16[17]{0:T(256)(128)(2,1)} %param.14) | copy-start | bytes 106
  6.5 14.6 %copy-start.4 = (bf16[17]{0:T(256)(128)(2,1)S(1)}, bf16[17]{0:T(256)(128)(2,1)}, u32[]{:S(2)}) copy-start(bf16[17]{0:T(256)(128)(2,1)} %param.15) | copy-start | bytes 106
  6.5 15.3 %copy-start.6 = (f32[1,8,256]{2,1,0:T(8,128)S(1)}, f32[1,8,256]{2,1,0:T(8,128)}, u32[]{:S(2)}) copy-start(f32[1,8,256]{2,1,0:T(8,128)} %param.16) | copy-start | bytes 24580
  8.1 32.6 %collective-permute-start.2 = (bf16[20,1,16,720]{3,2,0,1:T(8,128)(2,1)S(1)}, bf16[20,1,16,720]{3,2,0,1:T(8,128)(2,1)}, u32[]{:S(2)}, u32[]{:S(2)}) collective-permute-start(bf16[20,1,16,720]{3,2,0,1:T(8,128)(2,1)S(1)} %get-tuple-element.115), channel_id=1, source_target_pairs={{0,4},{4,8},{8,12},{12,16},{16,20},{20,24},{24,28},{28,0},{1,5},{5... | collective-permute-start | bytes 1382408 | tf_op jit(solution)/shard_map/ppermute | solution.py:14
  9.9 30.7 %collective-permute-start.3 = (bf16[20,1,16,720]{3,2,0,1:T(8,128)(2,1)S(1)}, bf16[20,1,16,720]{3,2,0,1:T(8,128)(2,1)}, u32[]{:S(2)}, u32[]{:S(2)}) collective-permute-start(bf16[20,1,16,720]{3,2,0,1:T(8,128)(2,1)S(1)} %get-tuple-element.116), channel_id=1, source_target_pairs={{4,0},{8,4},{12,8},{16,12},{20,16},{24,20},{28,24},{0,28},{5,1},{9... | collective-permute-start | bytes 1382408 | tf_op jit(solution)/shard_map/ppermute | solution.py:17
  11.2 12.0 %all-to-all-start = ((s32[1,8,256]{2,0,1:T(1,128)}), s32[1,8,256]{2,0,1:T(1,128)S(1)}, u32[]{:S(2)}, u32[]{:S(2)}) async-start(s32[1,8,256]{2,0,1:T(1,128)} %copy.48), calls=%async_computation | async-start | bytes 16384 | tf_op jit(solution)/shard_map/all_to_all | solution.py:136
  18.3 109.7 %collective-permute-start = (bf16[20,1,16,720]{3,2,0,1:T(8,128)(2,1)}, bf16[20,1,16,720]{3,2,0,1:T(8,128)(2,1)}, u32[]{:S(2)}, u32[]{:S(2)}) collective-permute-start(bf16[20,1,16,720]{3,2,0,1:T(8,128)(2,1)} %get-tuple-element.117), channel_id=1, source_target_pairs={{0,4},{4,8},{8,12},{12,16},{16,20},{20,24},{24,28},{28,0},{1,5},{5... | collective-permute-start | bytes 1382408 | tf_op jit(solution)/shard_map/ppermute | solution.py:14
  19.8 108.2 %collective-permute-start.1 = (bf16[20,1,16,720]{3,2,0,1:T(8,128)(2,1)S(1)}, bf16[20,1,16,720]{3,2,0,1:T(8,128)(2,1)}, u32[]{:S(2)}, u32[]{:S(2)}) collective-permute-start(bf16[20,1,16,720]{3,2,0,1:T(8,128)(2,1)S(1)} %get-tuple-element.118), channel_id=1, source_target_pairs={{4,0},{8,4},{12,8},{16,12},{20,16},{24,20},{28,24},{0,28},{5,1},{9... | collective-permute-start | bytes 1382408 | tf_op jit(solution)/shard_map/ppermute | solution.py:17
  23.2 10.1 %all-to-all-start.1 = ((f32[1,8,256]{2,0,1:T(1,128)}), f32[1,8,256]{2,0,1:T(1,128)S(1)}, u32[]{:S(2)}, u32[]{:S(2)}) async-start(f32[1,8,256]{2,0,1:T(1,128)} %compare_select_fusion), calls=%async_computation.1 | async-start | bytes 16384 | tf_op jit(solution)/shard_map/all_to_all | solution.py:135
  33.4 7.2 %all-to-all-start.2 = ((f32[1,8,256]{2,0,1:T(1,128)}), f32[1,8,256]{2,0,1:T(1,128)S(1)}, u32[]{:S(2)}, u32[]{:S(2)}) async-start(f32[1,8,256]{2,0,1:T(1,128)} %copy.57), calls=%async_computation.2 | async-start | bytes 16384 | tf_op jit(solution)/shard_map/all_to_all | solution.py:134
  37.3 74.3 %all-reduce.4.cloned.1.call-start = ((), (), s32[]{:S(2)}) async-start(), calls=%async_computation.3 | async-start | bytes 294912 | tf_op jit(solution)/shard_map/psum | solution.py:145
  112.7 3.8 %copy-start.2 = (f32[45,720]{1,0:T(8,128)S(1)}, f32[45,720]{1,0:T(8,128)}, u32[]{:S(2)}) copy-start(f32[45,720]{1,0:T(8,128)} %custom-call) | copy-start | bytes 388804
  116.5 11.5 %copy-start.1 = (bf16[20,1,45,720]{3,2,1,0:T(8,128)(2,1)S(1)}, bf16[20,1,45,720]{3,2,1,0:T(8,128)(2,1)}, u32[]{:S(2)}) copy-start(bf16[20,1,45,720]{3,2,1,0:T(8,128)(2,1)} %param.13) | copy-start | bytes 3888004
  119.7 5.1 %collective-permute-start.4 = (f32[1,16,720]{2,1,0:T(8,128)S(1)}, f32[1,16,720]{2,1,0:T(8,128)S(1)}, u32[]{:S(2)}, u32[]{:S(2)}) collective-permute-start(f32[1,16,720]{2,1,0:T(8,128)S(1)} %get-tuple-element.119), channel_id=1, source_target_pairs={{0,4},{4,8},{8,12},{12,16},{16,20},{20,24},{24,28},{28,0},{1,5},{5... | collective-permute-start | bytes 138248 | tf_op jit(solution)/shard_map/ppermute | solution.py:14
  123.5 4.4 %collective-permute-start.5 = (f32[1,16,720]{2,1,0:T(8,128)S(1)}, f32[1,16,720]{2,1,0:T(8,128)S(1)}, u32[]{:S(2)}, u32[]{:S(2)}) collective-permute-start(f32[1,16,720]{2,1,0:T(8,128)S(1)} %get-tuple-element.120), channel_id=1, source_target_pairs={{4,0},{8,4},{12,8},{16,12},{20,16},{24,20},{28,24},{0,28},{5,1},{9... | collective-permute-start | bytes 138248 | tf_op jit(solution)/shard_map/ppermute | solution.py:17
Sparse Core Ops, SparseCore 0:
  79.0 32.5 all-reduce.3
where the time goes:
time: 178 us; the launch traced here: 177 us
  matrix products  54 us (30%)
  waiting for transfers between devices  46.7 us (26%)
  local copies, waits for them, and re-layouts  37 us (21%)
  starting transfers between devices  20.5 us (12%)
  between operations  13.7 us (8%)
  other arithmetic  4.93 us (3%)
    psum x1, waiting for transfers between devices, local(): increment = lax.psum(member_sum, 'mem')  32.7 us
    dot_general x2, matrix products, localize(): jnp.einsum('ij,mljk->mlik', band_lon, extended, preferred_element_type=jn...  24.4 us
    dot_general x2, matrix products, localize(): jnp.einsum('mlibk,kq->mlibq', windows, band_blocks, preferred_element_typ...  23 us
    dot_general x2, local copies, waits for them, and re-layouts, localize(): jnp.einsum('mlibk,kq->mlibq', windows, band_blocks, preferred_element_typ...  12.8 us
    reshape x2, local copies, waits for them, and re-layouts, localize(): return result.reshape(members_here, levels, lon_cells, lat_cells)  9.75 us
    ppermute x3, starting transfers between devices, extended_2(): lax.ppermute(lax.slice_in_dim(block, block.shape[dim] - width, None, axis...  7.17 us
    all_to_all x1, waiting for transfers between devices, local(): lax.all_to_all(weights, 'tile', split_axis=1, concat_axis=0, tiled=True)  5.65 us
    all_to_all x1, starting transfers between devices, local(): lax.all_to_all(cell_index, 'tile', split_axis=1, concat_axis=0, tiled=True)  4.92 us
  transfers between devices with their start and end apart: 10, of which 6 were waited for; matrix products, arithmetic and copies ran while one was open for 30% of the time, Pallas kernels for 0%

commit v1 on v0

--- a/solution.py
+++ b/solution.py
@@ -3,6 +3,30 @@
 import jax.numpy as jnp
 from jax import lax
 from jax.sharding import PartitionSpec as P
+
+
+def split_up(array, dim, size):
+    shape = array.shape
+    blocks = array.reshape(*shape[:dim], size, shape[dim] // size, *shape[dim + 1 :])
+    return jnp.moveaxis(blocks, dim, 0)
+
+
+def in_order(tiles, dim):
+    tiles = jnp.moveaxis(tiles, 0, dim)
+    shape = tiles.shape
+    return tiles.reshape(*shape[:dim], shape[dim] * shape[dim + 1], *shape[dim + 2 :])
+
+
+def rotated_exchange(value, axis, split_dim, concat_dim):
+    devices, place = (lax.axis_size(axis), lax.axis_index(axis))
+    tiles = split_up(value, split_dim, devices)
+    out = tiles
+    for turn in range(1, devices):
+        target, source = ((place + turn) % devices, (place - turn) % devices)
+        sent = lax.dynamic_index_in_dim(tiles, target, 0)
+        received = lax.ppermute(sent, axis, [(i, (i + turn) % devices) for i in range(devices)])
+        out = lax.dynamic_update_slice_in_dim(out, received, source, axis=0)
+    return in_order(out, concat_dim)
 
 
 def extended_2(block, sides, width):
@@ -133,7 +157,7 @@
     received = (
         lax.all_to_all(innov, "tile", split_axis=1, concat_axis=0, tiled=True),
         lax.all_to_all(weights, "tile", split_axis=1, concat_axis=0, tiled=True),
-        lax.all_to_all(cell_index, "tile", split_axis=1, concat_axis=0, tiled=True),
+        rotated_exchange(cell_index, "tile", 1, 0),
     )
     observed = received[0].reshape(-1)
     weight_recv = received[1].reshape(-1)

time: 178 us -> 171 us (0.961)
  waiting for transfers between devices: 46.7 us -> 33.6 us
  starting transfers between devices: 20.5 us -> 23.4 us
  local copies, waits for them, and re-layouts: 37 us -> 39.2 us
    psum x1, waiting for transfers between devices: 32.7 us -> 24.9 us  [local(): increment = lax.psum(member_sum, 'mem')]
    all_to_all x1, waiting for transfers between devices: 5.65 us -> 0.01 us  [local(): lax.all_to_all(weights, 'tile', split_axis=1, concat_axis=0, tiled=True)]
    ppermute x0 -> x7, starting transfers between devices: none -> 5.03 us  [rotated_exchange(): lax.ppermute(sent, axis, [(i, (i + turn) % devices) for i in range(device...]
    all_to_all x1 -> x0, starting transfers between devices: 4.92 us -> none  [local(): lax.all_to_all(cell_index, 'tile', split_axis=1, concat_axis=0, tiled=True)]
    slice x2, local copies, waits for them, and re-layouts: 1.41 us -> 3.97 us  [band_from(): band = band + jnp.where(offsets == offset, taps[offset], 0.0)]
  transfers between devices with their start and end apart: 10 -> 16, of which waited for: 6 -> 6; matrix products, arithmetic and copies ran while one was open for 30% -> 32% of each run, Pallas kernels for 0% -> 0%
where the time goes in v1:
time: 171 us; the launch traced here: 170 us
  matrix products  54.3 us (32%)
  local copies, waits for them, and re-layouts  39.2 us (23%)
  waiting for transfers between devices  33.6 us (20%)
  starting transfers between devices  23.4 us (14%)
  between operations  13.7 us (8%)
  other arithmetic  5.54 us (3%)
    dot_general x2, matrix products, localize(): jnp.einsum('ij,mljk->mlik', band_lon, extended, preferred_element_type=jn...  25.2 us
    psum x1, waiting for transfers between devices, local(): increment = lax.psum(member_sum, 'mem')  24.9 us
    dot_general x2, matrix products, localize(): jnp.einsum('mlibk,kq->mlibq', windows, band_blocks, preferred_element_typ...  22.5 us
    dot_general x2, local copies, waits for them, and re-layouts, localize(): jnp.einsum('mlibk,kq->mlibq', windows, band_blocks, preferred_element_typ...  12.8 us
    reshape x2, local copies, waits for them, and re-layouts, localize(): return result.reshape(members_here, levels, lon_cells, lat_cells)  9.75 us
    ppermute x3, starting transfers between devices, extended_2(): lax.ppermute(lax.slice_in_dim(block, block.shape[dim] - width, None, axis...  8.32 us
    all_to_all x1, starting transfers between devices, local(): lax.all_to_all(innov, 'tile', split_axis=1, concat_axis=0, tiled=True)  5.05 us
    ppermute x7, starting transfers between devices, rotated_exchange(): lax.ppermute(sent, axis, [(i, (i + turn) % devices) for i in range(device...  5.03 us
  transfers between devices with their start and end apart: 16, of which 6 were waited for; matrix products, arithmetic and copies ran while one was open for 32% of the time, Pallas kernels for 0%

profile of v1, /device:TPU:11, one launch (start us, length us, event | category | flops | bytes accessed | tf_op | source)
XLA Modules:
  0.0 169.9 jit_solution(9055866673311708937)
XLA Ops:
  7.4 1.4 fusion.173
  9.5 2.0 %collective-permute-start.9 = (bf16[20,1,16,720]{3,2,0,1:T(8,128)(2,1)S(1)}, bf16[20,1,16,720]{3,2,0,1:T(8,128)(2,1)}, u32[]{:S(2)}, u32[]{:S(2)}) collective-permute-start(bf16[20,1,16,720]{3,2,0,1:T(8,128)(2,1)S(1)} %get-tuple-element.113), channel_id=1, source_target_pairs={{0,4},{4,8},{8,12},{12,16},{16,20},{20,24},{24,28},{28,0},{1,5},{5... | collective-permute-start | bytes 1382408 | tf_op jit(solution)/shard_map/ppermute | solution.py:38
  13.2 1.4 compare_select_fusion
  14.5 4.2 %all-to-all-start = ((f32[1,8,256]{2,0,1:T(1,128)}), f32[1,8,256]{2,0,1:T(1,128)S(1)}, u32[]{:S(2)}, u32[]{:S(2)}) async-start(f32[1,8,256]{2,0,1:T(1,128)} %compare_select_fusion), calls=%async_computation | async-start | bytes 16384 | tf_op jit(solution)/shard_map/all_to_all | solution.py:159
  18.7 2.0 %fusion.177 = (f32[1]{0:T(128)}, f32[1]{0:T(128)}, f32[1]{0:T(128)}, f32[1]{0:T(128)}, f32[1]{0:T(128)}, /*index=5*/f32[1]{0:T(128)}, f32[1]{0:T(128)}, f32[1]{0...) fusion(bf16[17]{0:T(256)(128)(2,1)} %param.14), kind=kLoop, calls=%fused_computation.217 | loop fusion | bytes 136 | tf_op jit(solution)/shard_map/slice | solution.py:51
  20.7 2.0 %fusion.176 = (f32[1]{0:T(128)}, f32[1]{0:T(128)}, f32[1]{0:T(128)}, f32[1]{0:T(128)}, f32[1]{0:T(128)}, /*index=5*/f32[1]{0:T(128)}, f32[1]{0:T(128)}, f32[1]{0...) fusion(bf16[17]{0:T(256)(128)(2,1)} %param.15), kind=kLoop, calls=%fused_computation.216 | loop fusion | bytes 136 | tf_op jit(solution)/shard_map/slice | solution.py:51
  22.7 2.2 %fusion.174 = (bf16[20,1,16,720]{3,2,0,1:T(8,128)(2,1)}, bf16[20,1,16,720]{3,2,0,1:T(8,128)(2,1)S(1)}) fusion(bf16[20,1,45,720]{3,2,0,1:T(8,128)(2,1)} %bitcast.174), kind=kLoop, calls=%fused_computation.214 | loop fusion | bytes 1843200 | tf_op jit(solution)/shard_map/slice | solution.py:39
  24.9 1.2 collective-permute-start.5
  29.1 2.5 %collective-permute-start = (bf16[20,1,16,720]{3,2,0,1:T(8,128)(2,1)}, bf16[20,1,16,720]{3,2,0,1:T(8,128)(2,1)}, u32[]{:S(2)}, u32[]{:S(2)}) collective-permute-start(bf16[20,1,16,720]{3,2,0,1:T(8,128)(2,1)} %get-tuple-element.115), channel_id=1, source_target_pairs={{0,4},{4,8},{8,12},{12,16},{16,20},{20,24},{24,28},{28,0},{1,5},{5... | collective-permute-start | bytes 1382408 | tf_op jit(solution)/shard_map/ppermute | solution.py:38
  32.7 12.5 %fusion.31 = bf16[20,1,45,720]{3,2,0,1:T(8,128)(2,1)S(1)} fusion(bf16[20,1,16,720]{3,2,0,1:T(8,128)(2,1)} %collective-permute-done.10, bf16[20,1,45,720]{3,2,0,1:T(8,128)(2,1)S(1)} %bitcast.173, bf16[20,1,16,720]{3,2,0,1:T(8,128)(2,1)} %collective-permute-done.9, f32[]{:T(128)} %bitcast.39, f32[]{:T(128)} %bitcast.38, f32[]{:T(128)} %bitcast.37, ...), kind=kOutput, calls=%fused_computation.44 | convolution fusion | flops 107279912 | bytes 3513668 | tf_op jit(solution)/shard_map/ij,mljk->mlik/dot_general | solution.py:70
  46.1 11.3 %fusion.25 = f32[20,45,5,144]{3,1,2,0:T(8,128)S(1)} fusion(f32[]{:T(128)} %bitcast.66, f32[]{:T(128)} %bitcast.65, f32[]{:T(128)} %bitcast.64, f32[]{:T(128)} %bitcast.63, f32[]{:T(128)} %bitcast.62, f32[]{:T(128)} %bitcast.61, f32[]{:T(128)} %bitcast.60, f32[]{:T(128)} %bitcast.59, f32[]{:T(128)} %bitcast.58, f32[]{:T(128)} %bitcast.57, f32[]{:T(128)} %bitcast.56, ...), kind=kOutput, calls=%fused_computation.38 | convolution fusion | flops 229439232 | bytes 4176772 | tf_op jit(solution)/shard_map/mlibk,kq->mlibq/dot_general | solution.py:83
  57.4 6.4 %copy.53 = f32[20,45,5,144]{3,2,1,0:T(8,128)} copy(f32[20,45,5,144]{3,1,2,0:T(8,128)S(1)} %fusion.25) | data formatting | bytes 5184000 | tf_op jit(solution)/shard_map/mlibk,kq->mlibq/dot_general | solution.py:83
  63.8 4.9 %reshape.138 = f32[20,1,45,720]{3,2,0,1:T(8,128)S(1)} reshape(f32[20,45,5,144]{3,2,1,0:T(8,128)} %copy.53) | data formatting | bytes 5184000 | tf_op jit(solution)/shard_map/reshape | solution.py:84
  68.7 2.4 %multiply_reduce_fusion = f32[45,720]{1,0:T(8,128)} fusion(f32[20,1,45,720]{3,2,0,1:T(8,128)S(1)} %reshape.138, bf16[20,1,45,720]{3,2,1,0:T(8,128)(2,1)} %param.13), kind=kLoop, calls=%fused_computation.22 | loop fusion | flops 1911600 | bytes 4017600 | tf_op jit(solution)/shard_map/reduce_sum | solution.py:153
  71.1 5.1 %all-to-all-start.1 = ((f32[1,8,256]{2,0,1:T(1,128)}), f32[1,8,256]{2,0,1:T(1,128)S(1)}, u32[]{:S(2)}, u32[]{:S(2)}) async-start(f32[1,8,256]{2,0,1:T(1,128)} %copy.55), calls=%async_computation.1 | async-start | bytes 16384 | tf_op jit(solution)/shard_map/all_to_all | solution.py:158
  76.2 3.3 %all-to-all-done.1 = f32[1,8,256]{2,0,1:T(1,128)S(1)} async-done(((f32[1,8,256]{2,0,1:T(1,128)}), f32[1,8,256]{2,0,1:T(1,128)S(1)}, u32[]{:S(2)}, u32[]{:S(2)}) %all-to-all-start.1) | async-done | bytes 8224 | tf_op jit(solution)/shard_map/all_to_all | solution.py:158
  79.5 24.9 %all-reduce.4.cloned.1.call-done = f32[720,45]{0,1:T(8,128)} async-done(((f32[720,45]{0,1:T(8,128)}), f32[720,45]{0,1:T(8,128)}) %all-reduce.4.cloned.1.call-update) | async-done | bytes 129616 | tf_op jit(solution)/shard_map/psum | solution.py:169
  105.6 3.8 %while.21 = (s32[]{:T(128)}, f32[2,1024]{1,0:T(2,128)S(1)}, s32[2,1024]{1,0:T(2,128)S(1)}, s32[2,1024]{1,0:T(2,128)S(1)}, f32[720,45]{1,0:T(8,128)S(1)}, /*index=5*/s32[]{:T(128)}, s32[]{:T(128)}) while((s32[]{:T(128)}, f32[2,1024]{1,0:T(2,128)S(1)}, s32[2,1024]{1,0:T(2,128)S(1)}, s32[2,1024]{1,0:T(2,128)S(1)}, f32[720,45]{1,0:T(8,128)S(1)}, ...), condition=%wide.region_4.5_spmd, body=%wide.region_2.4_spmd.sunk | while | flops 399005696 | bytes 166549 | solution.py:107
  105.6 1.8 %fusion.186 = f32[1024]{0:T(1024)S(1)} fusion(f32[720,45]{1,0:T(8,128)S(1)} %get-tuple-element.252, s32[1024]{0:T(1024)S(1)} %bitcast.184, s32[1024]{0:T(1024)S(1)} %bitcast.185), kind=kOutput, calls=%fused_computation.4.clone.1 | convolution fusion | flops 399005696 | bytes 141888 | tf_op jit(solution)/shard_map/while/body/eval_jaxpr/dot_general | solution.py:99
  107.5 1.8 %fusion.186 = f32[1024]{0:T(1024)S(1)} fusion(f32[720,45]{1,0:T(8,128)S(1)} %get-tuple-element.252, s32[1024]{0:T(1024)S(1)} %bitcast.184, s32[1024]{0:T(1024)S(1)} %bitcast.185), kind=kOutput, calls=%fused_computation.4.clone.1 | convolution fusion | flops 399005696 | bytes 141888 | tf_op jit(solution)/shard_map/while/body/eval_jaxpr/dot_general | solution.py:99
  109.4 3.1 %while.22 = (s32[]{:T(128)}, f32[45,720]{1,0:T(8,128)S(1)}, s32[2,1024]{1,0:T(2,128)S(1)}, f32[2,1024]{1,0:T(2,128)S(1)}, s32[2,1024]{1,0:T(2,128)S(1)}, /*index=5*/s32[]{:T(128)}, s32[]{:T(128)}) while((s32[]{:T(128)}, f32[45,720]{1,0:T(8,128)S(1)}, s32[2,1024]{1,0:T(2,128)S(1)}, f32[2,1024]{1,0:T(2,128)S(1)}, ...), condition=%wide.region_6.7_spmd.clone, body=%wide.region_5.6_spmd.clone.sunk | while | flops 399025440 | bytes 296159 | solution.py:141
  109.5 1.5 fusion.188
  111.0 1.5 fusion.188
  112.5 3.9 %collective-permute-start.11 = (f32[1,16,720]{2,1,0:T(8,128)S(1)}, f32[1,16,720]{2,1,0:T(8,128)S(1)}, u32[]{:S(2)}, u32[]{:S(2)}) collective-permute-start(f32[1,16,720]{2,1,0:T(8,128)S(1)} %get-tuple-element.117), channel_id=1, source_target_pairs={{0,4},{4,8},{8,12},{12,16},{16,20},{20,24},{24,28},{28,0},{1,5},{5... | collective-permute-start | bytes 138248 | tf_op jit(solution)/shard_map/ppermute | solution.py:38
  116.4 1.2 collective-permute-done.11
  117.6 3.2 %collective-permute-done.12 = f32[1,16,720]{2,1,0:T(8,128)S(1)} collective-permute-done((f32[1,16,720]{2,1,0:T(8,128)S(1)}, f32[1,16,720]{2,1,0:T(8,128)S(1)}, u32[]{:S(2)}, u32[]{:S(2)}) %collective-permute-start.12) | collective-permute-done | bytes 46112 | tf_op jit(solution)/shard_map/ppermute | solution.py:41
  120.9 12.7 %fusion.30 = bf16[20,1,45,720]{3,2,0,1:T(8,128)(2,1)S(1)} fusion(bf16[20,16,720]{2,1,0:T(8,128)(2,1)} %bitcast.8, bf16[20,45,720]{2,1,0:T(8,128)(2,1)S(1)} %bitcast.175, bf16[20,16,720]{2,1,0:T(8,128)(2,1)} %bitcast.5, f32[77,720]{1,0:T(8,128)S(1)} %maximum_bitcast_fusion.6, f32[]{:T(128)} %bitcast.39, f32[]{:T(128)} %bitcast.38, f32[]{:T(128)} %bitcast.37, ...), kind=kOutput, calls=%fused_computation.43 | convolution fusion | flops 109497512 | bytes 3735428 | tf_op jit(solution)/shard_map/ij,mljk->mlik/dot_general | solution.py:70
  134.5 11.3 %fusion.23 = f32[20,45,5,144]{3,1,2,0:T(8,128)S(1)} fusion(f32[]{:T(128)} %bitcast.66, f32[]{:T(128)} %bitcast.65, f32[]{:T(128)} %bitcast.64, f32[]{:T(128)} %bitcast.63, f32[]{:T(128)} %bitcast.62, f32[]{:T(128)} %bitcast.61, f32[]{:T(128)} %bitcast.60, f32[]{:T(128)} %bitcast.59, f32[]{:T(128)} %bitcast.58, f32[]{:T(128)} %bitcast.57, f32[]{:T(128)} %bitcast.56, ...), kind=kOutput, calls=%fused_computation.36 | convolution fusion | flops 229439232 | bytes 4176772 | tf_op jit(solution)/shard_map/mlibk,kq->mlibq/dot_general | solution.py:83
  145.8 6.4 %copy.57 = f32[20,45,5,144]{3,2,1,0:T(8,128)} copy(f32[20,45,5,144]{3,1,2,0:T(8,128)S(1)} %fusion.23) | data formatting | bytes 5184000 | tf_op jit(solution)/shard_map/mlibk,kq->mlibq/dot_general | solution.py:83
  152.2 4.9 %reshape.143 = f32[20,1,45,720]{3,2,0,1:T(8,128)S(1)} reshape(f32[20,45,5,144]{3,2,1,0:T(8,128)} %copy.57) | data formatting | bytes 5184000 | tf_op jit(solution)/shard_map/reshape | solution.py:84
  157.0 1.7 convert_add_fusion
  158.7 4.4 %copy.58 = f32[20,1,45,720]{3,1,2,0:T(1,128)} copy(f32[20,1,45,720]{3,2,0,1:T(8,128)S(1)} %convert_add_fusion) | data formatting | bytes 5184000 | tf_op jit(solution)/shard_map/add | solution.py:177
  (76 shorter events, 10.5 us)
Async XLA Ops:
  6.5 26.2 %copy-start = (bf16[20,1,45,720]{3,2,1,0:T(8,128)(2,1)S(1)}, bf16[20,1,45,720]{3,2,1,0:T(8,128)(2,1)}, u32[]{:S(2)}) copy-start(bf16[20,1,45,720]{3,2,1,0:T(8,128)(2,1)} %param.12) | copy-start | bytes 3888004
  6.5 21.6 %copy-start.3 = (f32[1,8,256]{2,1,0:T(8,128)S(1)}, f32[1,8,256]{2,1,0:T(8,128)}, u32[]{:S(2)}) copy-start(f32[1,8,256]{2,1,0:T(8,128)} %param.16) | copy-start | bytes 24580
  8.8 24.0 %collective-permute-start.10 = (bf16[20,1,16,720]{3,2,0,1:T(8,128)(2,1)S(1)}, bf16[20,1,16,720]{3,2,0,1:T(8,128)(2,1)}, u32[]{:S(2)}, u32[]{:S(2)}) collective-permute-start(bf16[20,1,16,720]{3,2,0,1:T(8,128)(2,1)S(1)} %get-tuple-element.114), channel_id=1, source_target_pairs={{4,0},{8,4},{12,8},{16,12},{20,16},{24,20},{28,24},{0,28},{5,1},{9... | collective-permute-start | bytes 1382408 | tf_op jit(solution)/shard_map/ppermute | solution.py:41
  9.5 23.2 %collective-permute-start.9 = (bf16[20,1,16,720]{3,2,0,1:T(8,128)(2,1)S(1)}, bf16[20,1,16,720]{3,2,0,1:T(8,128)(2,1)}, u32[]{:S(2)}, u32[]{:S(2)}) collective-permute-start(bf16[20,1,16,720]{3,2,0,1:T(8,128)(2,1)S(1)} %get-tuple-element.113), channel_id=1, source_target_pairs={{0,4},{4,8},{8,12},{12,16},{16,20},{20,24},{24,28},{28,0},{1,5},{5... | collective-permute-start | bytes 1382408 | tf_op jit(solution)/shard_map/ppermute | solution.py:38
  11.5 13.4 %collective-permute-start.2 = (s32[1,1,1,256]{3,0,2,1:T(1,128)S(1)}, s32[1,1,1,256]{3,0,2,1:T(1,128)S(1)}, u32[]{:S(2)}, u32[]{:S(2)}) collective-permute-start(s32[1,1,1,256]{3,0,2,1:T(1,128)S(1)} %get-tuple-element.128), channel_id=1, source_target_pairs={{0,4},{4,8},{8,12},{12,16},{16,20},{20,24},{24,28},{28,0},{1,5},{5... | collective-permute-start | bytes 3080 | tf_op jit(solution)/shard_map/ppermute | solution.py:27
  11.5 14.6 %collective-permute-start.3 = (s32[1,1,1,256]{3,0,2,1:T(1,128)S(1)}, s32[1,1,1,256]{3,0,2,1:T(1,128)S(1)}, u32[]{:S(2)}, u32[]{:S(2)}) collective-permute-start(s32[1,1,1,256]{3,0,2,1:T(1,128)S(1)} %get-tuple-element.127), channel_id=1, source_target_pairs={{0,8},{4,12},{8,16},{12,20},{16,24},{20,28},{24,0},{28,4},{1,9},{5... | collective-permute-start | bytes 3080 | tf_op jit(solution)/shard_map/ppermute | solution.py:27
  12.4 14.6 %collective-permute-start.4 = (s32[1,1,1,256]{3,0,2,1:T(1,128)S(1)}, s32[1,1,1,256]{3,0,2,1:T(1,128)S(1)}, u32[]{:S(2)}, u32[]{:S(2)}) collective-permute-start(s32[1,1,1,256]{3,0,2,1:T(1,128)S(1)} %get-tuple-element.126), channel_id=1, source_target_pairs={{0,12},{4,16},{8,20},{12,24},{16,28},{20,0},{24,4},{28,8},{1,13},{... | collective-permute-start | bytes 3080 | tf_op jit(solution)/shard_map/ppermute | solution.py:27
  14.5 56.5 %all-to-all-start = ((f32[1,8,256]{2,0,1:T(1,128)}), f32[1,8,256]{2,0,1:T(1,128)S(1)}, u32[]{:S(2)}, u32[]{:S(2)}) async-start(f32[1,8,256]{2,0,1:T(1,128)} %compare_select_fusion), calls=%async_computation | async-start | bytes 16384 | tf_op jit(solution)/shard_map/all_to_all | solution.py:159
  18.7 85.7 %all-reduce.4.cloned.1.call-start = ((), (), s32[]{:S(2)}) async-start(), calls=%async_computation.2 | async-start | bytes 294912 | tf_op jit(solution)/shard_map/psum | solution.py:169
  24.9 3.8 %collective-permute-start.5 = (s32[1,1,1,256]{3,0,2,1:T(1,128)S(1)}, s32[1,1,1,256]{3,0,2,1:T(1,128)S(1)}, u32[]{:S(2)}, u32[]{:S(2)}) collective-permute-start(s32[1,1,1,256]{3,0,2,1:T(1,128)S(1)} %get-tuple-element.125), channel_id=1, source_target_pairs={{0,16},{4,20},{8,24},{12,28},{16,0},{20,4},{24,8},{28,12},{1,17},{... | collective-permute-start | bytes 3080 | tf_op jit(solution)/shard_map/ppermute | solution.py:27
  26.1 3.0 %collective-permute-start.6 = (s32[1,1,1,256]{3,0,2,1:T(1,128)S(1)}, s32[1,1,1,256]{3,0,2,1:T(1,128)S(1)}, u32[]{:S(2)}, u32[]{:S(2)}) collective-permute-start(s32[1,1,1,256]{3,0,2,1:T(1,128)S(1)} %get-tuple-element.124), channel_id=1, source_target_pairs={{0,20},{4,24},{8,28},{12,0},{16,4},{20,8},{24,12},{28,16},{1,21},{... | collective-permute-start | bytes 3080 | tf_op jit(solution)/shard_map/ppermute | solution.py:27
  26.9 4.7 %collective-permute-start.7 = (s32[1,1,1,256]{3,0,2,1:T(1,128)S(1)}, s32[1,1,1,256]{3,0,2,1:T(1,128)S(1)}, u32[]{:S(2)}, u32[]{:S(2)}) collective-permute-start(s32[1,1,1,256]{3,0,2,1:T(1,128)S(1)} %get-tuple-element.129), channel_id=1, source_target_pairs={{0,24},{4,28},{8,0},{12,4},{16,8},{20,12},{24,16},{28,20},{1,25},{... | collective-permute-start | bytes 3080 | tf_op jit(solution)/shard_map/ppermute | solution.py:27
  28.7 3.9 %collective-permute-start.8 = (s32[1,1,1,256]{3,0,2,1:T(1,128)S(1)}, s32[1,1,1,256]{3,0,2,1:T(1,128)S(1)}, u32[]{:S(2)}, u32[]{:S(2)}) collective-permute-start(s32[1,1,1,256]{3,0,2,1:T(1,128)S(1)} %get-tuple-element.123), channel_id=1, source_target_pairs={{0,28},{4,0},{8,4},{12,8},{16,12},{20,16},{24,20},{28,24},{1,29},{... | collective-permute-start | bytes 3080 | tf_op jit(solution)/shard_map/ppermute | solution.py:27
  29.1 91.8 %collective-permute-start = (bf16[20,1,16,720]{3,2,0,1:T(8,128)(2,1)}, bf16[20,1,16,720]{3,2,0,1:T(8,128)(2,1)}, u32[]{:S(2)}, u32[]{:S(2)}) collective-permute-start(bf16[20,1,16,720]{3,2,0,1:T(8,128)(2,1)} %get-tuple-element.115), channel_id=1, source_target_pairs={{0,4},{4,8},{8,12},{12,16},{16,20},{20,24},{24,28},{28,0},{1,5},{5... | collective-permute-start | bytes 1382408 | tf_op jit(solution)/shard_map/ppermute | solution.py:38
  31.6 89.3 %collective-permute-start.1 = (bf16[20,1,16,720]{3,2,0,1:T(8,128)(2,1)S(1)}, bf16[20,1,16,720]{3,2,0,1:T(8,128)(2,1)}, u32[]{:S(2)}, u32[]{:S(2)}) collective-permute-start(bf16[20,1,16,720]{3,2,0,1:T(8,128)(2,1)S(1)} %get-tuple-element.116), channel_id=1, source_target_pairs={{4,0},{8,4},{12,8},{16,12},{20,16},{24,20},{28,24},{0,28},{5,1},{9... | collective-permute-start | bytes 1382408 | tf_op jit(solution)/shard_map/ppermute | solution.py:41
  71.1 8.4 %all-to-all-start.1 = ((f32[1,8,256]{2,0,1:T(1,128)}), f32[1,8,256]{2,0,1:T(1,128)S(1)}, u32[]{:S(2)}, u32[]{:S(2)}) async-start(f32[1,8,256]{2,0,1:T(1,128)} %copy.55), calls=%async_computation.1 | async-start | bytes 16384 | tf_op jit(solution)/shard_map/all_to_all | solution.py:158
  105.6 3.8 %copy-start.2 = (f32[45,720]{1,0:T(8,128)S(1)}, f32[45,720]{1,0:T(8,128)}, u32[]{:S(2)}) copy-start(f32[45,720]{1,0:T(8,128)} %custom-call) | copy-start | bytes 388804
  109.4 11.5 %copy-start.1 = (bf16[20,1,45,720]{3,2,1,0:T(8,128)(2,1)S(1)}, bf16[20,1,45,720]{3,2,1,0:T(8,128)(2,1)}, u32[]{:S(2)}) copy-start(bf16[20,1,45,720]{3,2,1,0:T(8,128)(2,1)} %param.13) | copy-start | bytes 3888004
  112.5 5.1 %collective-permute-start.11 = (f32[1,16,720]{2,1,0:T(8,128)S(1)}, f32[1,16,720]{2,1,0:T(8,128)S(1)}, u32[]{:S(2)}, u32[]{:S(2)}) collective-permute-start(f32[1,16,720]{2,1,0:T(8,128)S(1)} %get-tuple-element.117), channel_id=1, source_target_pairs={{0,4},{4,8},{8,12},{12,16},{16,20},{20,24},{24,28},{28,0},{1,5},{5... | collective-permute-start | bytes 138248 | tf_op jit(solution)/shard_map/ppermute | solution.py:38
  116.4 4.4 %collective-permute-start.12 = (f32[1,16,720]{2,1,0:T(8,128)S(1)}, f32[1,16,720]{2,1,0:T(8,128)S(1)}, u32[]{:S(2)}, u32[]{:S(2)}) collective-permute-start(f32[1,16,720]{2,1,0:T(8,128)S(1)} %get-tuple-element.118), channel_id=1, source_target_pairs={{4,0},{8,4},{12,8},{16,12},{20,16},{24,20},{28,24},{0,28},{5,1},{9... | collective-permute-start | bytes 138248 | tf_op jit(solution)/shard_map/ppermute | solution.py:41
Sparse Core Ops, SparseCore 0:
  71.2 33.2 all-reduce.3
